TPU v7x, 32 devices: a whole 2x2x4 slice. The times are simulated.
32 devices in a mesh: groups: 2 (over y), bricks: 4 (over z), heads: 4 (over x, core).
Axes of the slice: x: 2, y: 2, z: 4, core: 2. Of those that a mesh axis runs over, the one named last changes fastest.
Arguments:
- voxel_feats: bfloat16 [4096, 1024], P(('groups', 'bricks'), 'heads'), parts along dimension 0, may hold values from -6 to 6
- face_open: int32 [8], P('groups'), parts along dimension 0, may hold values from 0 to 1
- pattern: int32 [8, 4], P('groups'), parts along dimension 0, may hold values from 0 to 1, as said below
- conv_weight: bfloat16 [27, 1024], P(None, 'heads'), may hold values from -1.25 to 1.25
- conv_bias: bfloat16 [1024], P('heads'), may hold values from -0.5 to 0.5
- gain_one: bfloat16 [1024], replicated, may hold values from 0.099609375 to 1.8984375
- query_weight: bfloat16 [1024, 1024], P(None, 'heads'), may hold values from -3 to 3
- key_weight: bfloat16 [1024, 1024], P(None, 'heads'), may hold values from -3 to 3
- value_weight: bfloat16 [1024, 1024], P(None, 'heads'), may hold values from -0.1875 to 0.1875
- out_weight: bfloat16 [1024, 1024], P('heads'), may hold values from -0.1875 to 0.1875
- gain_two: bfloat16 [1024], replicated, may hold values from 0.099609375 to 1.8984375
- up_weight: bfloat16 [1024, 4096], P(None, 'heads'), may hold values from -0.1875 to 0.1875
- down_weight: bfloat16 [4096, 1024], P('heads'), may hold values from -0.09375 to 0.09375
Outputs:
- block_out: bfloat16 [4096, 1024], P(('groups', 'bricks'), 'heads'), parts along dimension 0
There are 2 independent parts, one for each index of `groups`. A program takes and returns all parts, laid end to end along the dimension named above; an argument that names none is the same for every part. Nothing has to cross between parts.
Inputs may be any that keep to these rules, and one draw needn't show every extreme that they name: pattern is 0 or 1; every brick attends to itself; each query brick attends to 3 or more key bricks, and some query brick to all 4.
All inputs are finite; a program needn't handle non-finite values.
Results may differ from a plain program's by a relative error of at most 0.012.
Values may be sent and summed in bfloat16 or wider, within the bound.
No kernel may reach another device: no remote copies, remote signals or barrier semaphores. Data moves between devices by JAX's collectives and lax.ppermute only.
A program may use at most 64 MiB of HBM per device.

v0:
```python
import jax
import jax.numpy as jnp
from jax import lax
from jax.sharding import PartitionSpec as P

EDGE = 8
HEAD_DIM = 64
epsilon = 1e-05


def extended_2(value, sides, width):
    for axis, dim in sides:
        size, length = (lax.axis_size(axis), value.shape[dim])
        up = [(i, (i + 1) % size) for i in range(size - 1)]
        down = [(j, i) for i, j in up]
        last = lax.slice_in_dim(value, length - width, length, axis=dim)
        first = lax.slice_in_dim(value, 0, width, axis=dim)
        before = lax.ppermute(last, axis, up)
        after = lax.ppermute(first, axis, down)
        value = jnp.concatenate([before, value, after], axis=dim)
    return value


def layer_norm(inputs, gain_vec):
    values = inputs.astype(jnp.float32)
    center = values - jnp.mean(values, axis=-1, keepdims=True)
    spread = jnp.mean(center * center, axis=-1, keepdims=True)
    return center * lax.rsqrt(spread + epsilon) * gain_vec.astype(jnp.float32)


def depthwise(brick_vals, lower_face, upper_face, conv_weight, conv_bias):
    brick_count = brick_vals.shape[0]
    edge_len = brick_vals.shape[1]
    channels = brick_vals.shape[3]
    layers = jnp.concatenate([lower_face[:, None], brick_vals, upper_face[:, None]], axis=1)
    layers = layers.reshape(brick_count, edge_len + 2, edge_len, edge_len, channels)
    padded = jnp.pad(layers, ((0, 0), (0, 0), (1, 1), (1, 1), (0, 0)))
    weights = conv_weight.astype(jnp.float32)
    summed = jnp.zeros((brick_count, edge_len, edge_len, edge_len, channels), jnp.float32)
    for step_x in range(3):
        for step_y in range(3):
            for step_z in range(3):
                window = padded[
                    :,
                    step_x : step_x + edge_len,
                    step_y : step_y + edge_len,
                    step_z : step_z + edge_len,
                ]
                summed = summed + weights[step_x * 9 + step_y * 3 + step_z] * window
    return summed.reshape(brick_count * edge_len**3, channels) + conv_bias.astype(jnp.float32)


def shards(
    voxel_feats,
    face_open,
    pattern,
    conv_weight,
    conv_bias,
    gain_one,
    query_weight,
    key_weight,
    value_weight,
    out_weight,
    gain_two,
    up_weight,
    down_weight,
):
    row_count = voxel_feats.shape[0]
    local_width = voxel_feats.shape[1]
    face_rows = EDGE * EDGE
    brick_rows = EDGE * face_rows
    local_bricks = row_count // brick_rows
    brick_total = pattern.shape[0]
    first_brick = lax.axis_index("bricks") * local_bricks
    extended = extended_2(voxel_feats, (("bricks", 0),), face_rows)
    brick_vals = extended[face_rows : face_rows + row_count].astype(jnp.float32)
    brick_vals = brick_vals.reshape(local_bricks, EDGE, face_rows, local_width)
    lower_face = jnp.concatenate(
        [extended[:face_rows].astype(jnp.float32)[None], brick_vals[:-1, EDGE - 1]], axis=0
    )
    upper_face = jnp.concatenate(
        [brick_vals[1:, 0], extended[face_rows + row_count :].astype(jnp.float32)[None]], axis=0
    )
    brick_ids = first_brick + jnp.arange(local_bricks, dtype=jnp.int32)
    lower_open = jnp.where(brick_ids >= 1, jnp.take(face_open, brick_ids), 0)
    upper_open = jnp.where(
        brick_ids + 1 < brick_total,
        jnp.take(face_open, jnp.minimum(brick_ids + 1, brick_total - 1)),
        0,
    )
    lower_face = lower_face * lower_open.astype(jnp.float32)[:, None, None]
    upper_face = upper_face * upper_open.astype(jnp.float32)[:, None, None]
    conv_out = depthwise(brick_vals, lower_face, upper_face, conv_weight, conv_bias)
    stream = (voxel_feats.astype(jnp.float32) + conv_out).astype(jnp.bfloat16)
    stream_full = lax.all_gather(stream, "heads", axis=1, tiled=True)
    normed = layer_norm(stream_full, gain_one).astype(jnp.bfloat16)
    queries = jnp.dot(normed, query_weight, preferred_element_type=jnp.float32).astype(jnp.bfloat16)
    head_count = local_width // HEAD_DIM
    query_heads = queries.reshape(local_bricks, brick_rows, head_count, HEAD_DIM)
    score_scale = HEAD_DIM ** (-0.5)
    start_state = (
        jnp.full((local_bricks, head_count, brick_rows), -1e30, jnp.float32),
        jnp.zeros((local_bricks, head_count, brick_rows), jnp.float32),
        jnp.zeros((local_bricks, brick_rows, head_count, HEAD_DIM), jnp.float32),
    )

    def absorb(state_in, local_id, key_brick, fetch_pair):
        linked = pattern[first_brick + local_id, key_brick]

        def include(state_now):
            row_max, row_mass, weighted = state_now
            key_rows, value_rows = fetch_pair()
            keys_h = key_rows.reshape(brick_rows, head_count, HEAD_DIM)
            values_h = value_rows.reshape(brick_rows, head_count, HEAD_DIM)
            query_one = lax.dynamic_index_in_dim(query_heads, local_id, 0, keepdims=False)
            scores = (
                jnp.einsum("qhd,khd->hqk", query_one, keys_h, preferred_element_type=jnp.float32)
                * score_scale
            )
            max_old = lax.dynamic_index_in_dim(row_max, local_id, 0, keepdims=False)
            mass_old = lax.dynamic_index_in_dim(row_mass, local_id, 0, keepdims=False)
            sum_old = lax.dynamic_index_in_dim(weighted, local_id, 0, keepdims=False)
            max_new = jnp.maximum(max_old, jnp.max(scores, axis=-1))
            factor = jnp.exp(max_old - max_new)
            weights = jnp.exp(scores - max_new[:, :, None])
            mass_new = mass_old * factor + jnp.sum(weights, axis=-1)
            sum_new = sum_old * jnp.transpose(factor)[:, :, None] + jnp.einsum(
                "hqk,khd->qhd",
                weights.astype(jnp.bfloat16),
                values_h,
                preferred_element_type=jnp.float32,
            )
            return (
                lax.dynamic_update_index_in_dim(row_max, max_new, local_id, 0),
                lax.dynamic_update_index_in_dim(row_mass, mass_new, local_id, 0),
                lax.dynamic_update_index_in_dim(weighted, sum_new, local_id, 0),
            )

        return lax.cond(linked > 0, include, lambda state_now: state_now, state_in)

    keys_all = jnp.dot(normed, key_weight, preferred_element_type=jnp.float32).astype(jnp.bfloat16)
    values_all = jnp.dot(normed, value_weight, preferred_element_type=jnp.float32).astype(
        jnp.bfloat16
    )
    key_piece = lax.all_gather(keys_all, "bricks", axis=0, tiled=True)
    value_piece = lax.all_gather(values_all, "bricks", axis=0, tiled=True)
    piece_bricks = key_piece.shape[0] // brick_rows

    def visit(visit_idx, state_now):
        local_id = visit_idx // piece_bricks
        offset = visit_idx % piece_bricks

        def fetch_pair():
            return (
                lax.dynamic_slice_in_dim(key_piece, offset * brick_rows, brick_rows, 0),
                lax.dynamic_slice_in_dim(value_piece, offset * brick_rows, brick_rows, 0),
            )

        return absorb(state_now, local_id, offset, fetch_pair)

    result = lax.fori_loop(0, local_bricks * piece_bricks, visit, start_state)
    row_max, row_mass, weighted = result
    attended = (weighted / jnp.transpose(row_mass, (0, 2, 1))[:, :, :, None]).astype(jnp.bfloat16)
    attended = attended.reshape(row_count, local_width)
    partial_out = jnp.dot(attended, out_weight, preferred_element_type=jnp.float32)
    full_sum = lax.psum(partial_out.astype(jnp.bfloat16), "heads").astype(jnp.float32)
    stream_two_full = (stream_full.astype(jnp.float32) + full_sum).astype(jnp.bfloat16)
    stream_two = lax.dynamic_slice_in_dim(
        stream_two_full, lax.axis_index("heads") * local_width, local_width, 1
    )
    normed_two = layer_norm(stream_two_full, gain_two).astype(jnp.bfloat16)
    hidden = jax.nn.gelu(
        jnp.dot(normed_two, up_weight, preferred_element_type=jnp.float32), approximate=True
    ).astype(jnp.bfloat16)
    lowered = jnp.dot(hidden, down_weight, preferred_element_type=jnp.float32)
    mixed = lax.psum_scatter(
        lowered.astype(jnp.bfloat16), "heads", scatter_dimension=1, tiled=True
    ).astype(jnp.float32)
    return (stream_two.astype(jnp.float32) + mixed).astype(jnp.bfloat16)


def solution(mesh):
    return jax.shard_map(
        shards,
        mesh=mesh,
        in_specs=(
            P(("groups", "bricks"), "heads"),
            P("groups"),
            P("groups", None),
            P(None, "heads"),
            P("heads"),
            P(),
            P(None, "heads"),
            P(None, "heads"),
            P(None, "heads"),
            P("heads", None),
            P(),
            P(None, "heads"),
            P("heads", None),
        ),
        out_specs=P(("groups", "bricks"), "heads"),
        check_vma=False,
    )
```

profile of v0, /device:TPU:0, one launch (start us, length us, event | category | flops | bytes accessed | tf_op | source)
XLA Modules:
  0.0 208.5 jit_solution(12115050096938499187)
XLA Ops:
  7.5 1.3 collective-permute-start.1
  8.8 5.6 %collective-permute-start = (bf16[64,256]{1,0:T(8,128)(2,1)S(1)}, bf16[64,256]{1,0:T(8,128)(2,1)S(1)}, u32[]{:S(2)}, u32[]{:S(2)}) collective-permute-start(bf16[64,256]{1,0:T(8,128)(2,1)S(1)} %get-tuple-element.350), channel_id=1, source_target_pairs={{0,4},{4,8},{8,12},{1,5},{5,9},{9,13},{2,6},{6,10},{10,14},{3,7},{... | collective-permute-start | bytes 98312 | tf_op jit(solution)/shard_map/ppermute | solution.py:18
  16.2 1.4 fusion.98
  20.9 1.6 fusion.57
  23.4 17.6 %all-gather.4.cloned.1.call-done = bf16[512,1024]{1,0:T(8,128)(2,1)} async-done(((bf16[512,256]{1,0:T(8,128)(2,1)}), bf16[512,1024]{1,0:T(8,128)(2,1)}) %all-gather.4.cloned.1.call-update) | async-done | bytes 1048592 | tf_op jit(solution)/shard_map/all_gather | solution.py:95
  41.0 1.5 convert_reduce_fusion
  42.5 1.6 fusion.25
  44.2 2.3 %convolution_convert_fusion.4 = bf16[512,256]{1,0:T(8,128)(2,1)} fusion(bf16[1024,256]{1,0:T(8,128)(2,1)} %param.24, bf16[512,1024]{1,0:T(8,128)(2,1)S(1)} %copy-done.1, f32[1024]{0:T(1024)S(1)} %convert_element_type.108, f32[512]{0:T(512)S(1)} %add_rsqrt_fusion.1, f32[512]{0:T(512)S(1)} %broadcast_multiply_fusion.1), kind=kOutput, calls=%fused_computation.61 | convolution fusion | flops 271187968 | bytes 1843200 | tf_op jit(solution)/shard_map/dot_general | solution.py:141
  46.5 2.3 %convolution_convert_fusion.2 = bf16[512,256]{1,0:T(8,128)(2,1)} fusion(bf16[1024,256]{1,0:T(8,128)(2,1)} %param.25, bf16[512,1024]{1,0:T(8,128)(2,1)S(1)} %copy-done.1, f32[1024]{0:T(1024)S(1)} %convert_element_type.108, f32[512]{0:T(512)S(1)} %add_rsqrt_fusion.1, f32[512]{0:T(512)S(1)} %broadcast_multiply_fusion.1), kind=kOutput, calls=%fused_computation.59 | convolution fusion | flops 271187968 | bytes 1843200 | tf_op jit(solution)/shard_map/dot_general | solution.py:142
  48.8 1.7 convolution_convert_fusion.3
  50.6 24.0 %all-gather.6.cloned.1.call-done = bf16[2048,256]{1,0:T(8,128)(2,1)} async-done(((bf16[512,256]{1,0:T(8,128)(2,1)}), bf16[2048,256]{1,0:T(8,128)(2,1)}) %all-gather.6.cloned.1.call-update) | async-done | bytes 1048592 | tf_op jit(solution)/shard_map/all_gather | solution.py:145
  74.5 2.3 %copy.15 = bf16[2048,256]{0,1:T(8,128)(2,1)} copy(bf16[2048,256]{1,0:T(8,128)(2,1)} %all-gather.6.cloned.1.call-done) | data formatting | bytes 2097152 | tf_op jit(solution)/shard_map/while | solution.py:161
  76.8 26.8 %all-gather.8.cloned.1.call-done = bf16[2048,256]{1,0:T(8,128)(2,1)} async-done(((bf16[512,256]{1,0:T(8,128)(2,1)}), bf16[2048,256]{1,0:T(8,128)(2,1)}) %all-gather.8.cloned.1.call-update) | async-done | bytes 1048592 | tf_op jit(solution)/shard_map/all_gather | solution.py:146
  103.6 2.3 %copy.16 = bf16[2048,256]{0,1:T(8,128)(2,1)} copy(bf16[2048,256]{1,0:T(8,128)(2,1)} %all-gather.8.cloned.1.call-done) | data formatting | bytes 2097152 | tf_op jit(solution)/shard_map/while | solution.py:161
  105.9 22.0 %while.21 = (s32[]{:T(128)}, f32[1,4,512]{2,1,0:T(4,128)S(1)}, f32[1,4,512]{2,1,0:T(4,128)S(1)}, f32[1,512,4,64]{1,3,2,0:T(8,128)S(1)}, s32[]{:T(128)}, /*index=...) while((s32[]{:T(128)}, f32[1,4,512]{2,1,0:T(4,128)S(1)}, ...), condition=%wide.region_7.8_spmd, body=%wide.region_2.0_spmd.sunk | while | flops 277094432 | bytes 15589916 | solution.py:161
  106.0 1.3 dynamic_slice.33
  107.9 3.5 %conditional.2 = ((f32[1,4,512]{2,1,0:T(4,128)S(1)}, f32[1,4,512]{2,1,0:T(4,128)S(1)}, f32[1,512,4,64]{1,3,2,0:T(8,128)S(1)})) conditional(s32[]{:T(128)} %bitcast.111, (f32[1,4,512]{2,1,0:T(4,128)S(1)}, f32[1,4,512]{2,1,0:T(4,128)S(1)}, f32[1,512,4,64]{1,3,2,0:T(8,128)S(1)}) %tuple.92, (s32[]{:T(128)}, bf16[2048,256]{0,1:T(8,128)(2,1)}, ...), branch_computations={%region_3.3_spmd, %region_4.6_spmd} | conditional | flops 277094400 | bytes 15589458 | solution.py:139
  107.9 1.1 constant_dynamic-slice_fusion
  111.5 1.3 dynamic_slice.33
  113.4 3.5 %conditional.2 = ((f32[1,4,512]{2,1,0:T(4,128)S(1)}, f32[1,4,512]{2,1,0:T(4,128)S(1)}, f32[1,512,4,64]{1,3,2,0:T(8,128)S(1)})) conditional(s32[]{:T(128)} %bitcast.111, (f32[1,4,512]{2,1,0:T(4,128)S(1)}, f32[1,4,512]{2,1,0:T(4,128)S(1)}, f32[1,512,4,64]{1,3,2,0:T(8,128)S(1)}) %tuple.92, (s32[]{:T(128)}, bf16[2048,256]{0,1:T(8,128)(2,1)}, ...), branch_computations={%region_3.3_spmd, %region_4.6_spmd} | conditional | flops 277094400 | bytes 15589458 | solution.py:139
  113.4 1.1 constant_dynamic-slice_fusion
  117.0 1.3 dynamic_slice.33
  118.9 3.5 %conditional.2 = ((f32[1,4,512]{2,1,0:T(4,128)S(1)}, f32[1,4,512]{2,1,0:T(4,128)S(1)}, f32[1,512,4,64]{1,3,2,0:T(8,128)S(1)})) conditional(s32[]{:T(128)} %bitcast.111, (f32[1,4,512]{2,1,0:T(4,128)S(1)}, f32[1,4,512]{2,1,0:T(4,128)S(1)}, f32[1,512,4,64]{1,3,2,0:T(8,128)S(1)}) %tuple.92, (s32[]{:T(128)}, bf16[2048,256]{0,1:T(8,128)(2,1)}, ...), branch_computations={%region_3.3_spmd, %region_4.6_spmd} | conditional | flops 277094400 | bytes 15589458 | solution.py:139
  118.9 1.1 constant_dynamic-slice_fusion
  122.5 1.3 dynamic_slice.33
  124.4 3.5 %conditional.2 = ((f32[1,4,512]{2,1,0:T(4,128)S(1)}, f32[1,4,512]{2,1,0:T(4,128)S(1)}, f32[1,512,4,64]{1,3,2,0:T(8,128)S(1)})) conditional(s32[]{:T(128)} %bitcast.111, (f32[1,4,512]{2,1,0:T(4,128)S(1)}, f32[1,4,512]{2,1,0:T(4,128)S(1)}, f32[1,512,4,64]{1,3,2,0:T(8,128)S(1)}) %tuple.92, (s32[]{:T(128)}, bf16[2048,256]{0,1:T(8,128)(2,1)}, ...), branch_computations={%region_3.3_spmd, %region_4.6_spmd} | conditional | flops 277094400 | bytes 15589458 | solution.py:139
  128.0 2.6 %convolution_convert_fusion.1 = bf16[512,1024]{1,0:T(8,128)(2,1)} fusion(bf16[512,256]{0,1:T(8,128)(2,1)S(1)} %bitcast.116, bf16[256,1024]{1,0:T(8,128)(2,1)} %param.26), kind=kOutput, calls=%fused_computation.58 | convolution fusion | flops 268959744 | bytes 1835008 | tf_op jit(solution)/shard_map/dot_general | solution.py:165
  130.7 35.7 %all-reduce.3.cloned.1.call-done = bf16[512,1024]{1,0:T(8,128)(2,1)} async-done(((bf16[512,1024]{1,0:T(8,128)(2,1)}), bf16[512,1024]{1,0:T(8,128)(2,1)}) %all-reduce.3.cloned.1.call-update) | async-done | bytes 1048592 | tf_op jit(solution)/shard_map/psum | solution.py:166
  166.4 1.6 convert_reduce_fusion.1
  169.4 5.4 %convolution_convert_fusion = bf16[512,1024]{1,0:T(8,128)(2,1)} fusion(bf16[1024,1024]{1,0:T(8,128)(2,1)S(1)} %copy-done, bf16[1024,1024]{1,0:T(8,128)(2,1)} %param.28, bf16[512,1024]{1,0:T(8,128)(2,1)} %copy-done.3, f32[1024]{0:T(1024)S(1)} %convert_element_type.119, f32[512]{0:T(512)S(1)} %add_rsqrt_fusion, f32[512]{0:T(512)S(1)} %broadcast_multiply_fusion), kind=kOutput, calls=%fused_computation.57 | convolution fusion | flops 2155347968 | bytes 6299648 | tf_op jit(solution)/shard_map/dot_general | solution.py:175
  174.8 25.4 %reduce-scatter.2.cloned.1.call-done = bf16[512,256]{1,0:T(8,128)(2,1)} async-done(((bf16[512,1024]{1,0:T(8,128)(2,1)}), bf16[512,256]{1,0:T(8,128)(2,1)}) %reduce-scatter.2.cloned.1.call-update) | async-done | bytes 262160 | tf_op jit(solution)/shard_map/reduce_scatter | solution.py:176
  200.2 1.8 add_convert_fusion
  (67 shorter events, 18.1 us)
Async XLA Ops:
  6.5 162.8 %copy-start = (bf16[1024,1024]{1,0:T(8,128)(2,1)S(1)}, bf16[1024,1024]{1,0:T(8,128)(2,1)}, u32[]{:S(2)}) copy-start(bf16[1024,1024]{1,0:T(8,128)(2,1)} %param.29) | copy-start | bytes 6291460
  6.5 34.4 %all-gather.4.cloned.1.call-start = ((), (), s32[]{:S(2)}) async-start(), calls=%async_computation.1 | async-start | bytes 1310720 | tf_op jit(solution)/shard_map/all_gather | solution.py:95
  7.5 13.1 %collective-permute-start.1 = (bf16[64,256]{1,0:T(8,128)(2,1)S(1)}, bf16[64,256]{1,0:T(8,128)(2,1)S(1)}, u32[]{:S(2)}, u32[]{:S(2)}) collective-permute-start(bf16[64,256]{1,0:T(8,128)(2,1)S(1)} %get-tuple-element.351), channel_id=1, source_target_pairs={{4,0},{8,4},{12,8},{5,1},{9,5},{13,9},{6,2},{10,6},{14,10},{7,3},{... | collective-permute-start | bytes 98312 | tf_op jit(solution)/shard_map/ppermute | solution.py:19
  8.8 11.8 %collective-permute-start = (bf16[64,256]{1,0:T(8,128)(2,1)S(1)}, bf16[64,256]{1,0:T(8,128)(2,1)S(1)}, u32[]{:S(2)}, u32[]{:S(2)}) collective-permute-start(bf16[64,256]{1,0:T(8,128)(2,1)S(1)} %get-tuple-element.350), channel_id=1, source_target_pairs={{0,4},{4,8},{8,12},{1,5},{5,9},{9,13},{2,6},{6,10},{10,14},{3,7},{... | collective-permute-start | bytes 98312 | tf_op jit(solution)/shard_map/ppermute | solution.py:18
  20.9 1.6 copy-start.4
  20.9 2.5 %copy-start.5 = (bf16[1024]{0:T(1024)(128)(2,1)S(1)}, bf16[1024]{0:T(1024)(128)(2,1)}, u32[]{:S(2)}) copy-start(bf16[1024]{0:T(1024)(128)(2,1)} %param.22) | copy-start | bytes 6148
  23.3 51.2 %all-gather.6.cloned.1.call-start = ((), (), s32[]{:S(2)}) async-start(), calls=%async_computation.2 | async-start | bytes 1310720 | tf_op jit(solution)/shard_map/all_gather | solution.py:145
  41.0 3.2 %copy-start.1 = (bf16[512,1024]{1,0:T(8,128)(2,1)S(1)}, bf16[512,1024]{1,0:T(8,128)(2,1)}, u32[]{:S(2)}) copy-start(bf16[512,1024]{1,0:T(8,128)(2,1)} %all-gather.4.cloned.1.call-done) | copy-start | bytes 3145732
  46.4 57.1 %all-gather.8.cloned.1.call-start = ((), (), s32[]{:S(2)}) async-start(), calls=%async_computation.3 | async-start | bytes 1310720 | tf_op jit(solution)/shard_map/all_gather | solution.py:146
  48.8 117.6 %all-reduce.3.cloned.1.call-start = ((), (), s32[]{:S(2)}) async-start(), calls=%async_computation.4 | async-start | bytes 2097152 | tf_op jit(solution)/shard_map/psum | solution.py:166
  127.9 2.7 %copy-start.6 = (bf16[1024]{0:T(1024)(128)(2,1)S(1)}, bf16[1024]{0:T(1024)(128)(2,1)}, u32[]{:S(2)}) copy-start(bf16[1024]{0:T(1024)(128)(2,1)} %param.27) | copy-start | bytes 6148
  128.0 38.3 %copy-start.2 = (bf16[512,1024]{1,0:T(8,128)(2,1)S(1)}, bf16[512,1024]{1,0:T(8,128)(2,1)}, u32[]{:S(2)}) copy-start(bf16[512,1024]{1,0:T(8,128)(2,1)} %all-gather.4.cloned.1.call-done) | copy-start | bytes 3145732
  130.6 69.5 %reduce-scatter.2.cloned.1.call-start = ((), (), s32[]{:S(2)}) async-start(), calls=%async_computation.5 | async-start | bytes 1310720 | tf_op jit(solution)/shard_map/reduce_scatter | solution.py:176
  168.0 1.0 copy-start.3
Sparse Core Ops, SparseCore 0:
  23.4 17.5 all-gather.3
  46.6 27.9 all-gather.5
  76.1 27.4 all-gather.7
  130.7 35.5 all-reduce.2
  174.9 25.2 reduce-scatter.1
where the time goes:
time: 209 us; the launch traced here: 208 us
  waiting for transfers between devices  129 us (62%)
  matrix products  21 us (10%)
  local copies, waits for them, and re-layouts  19.2 us (9%)
  between operations  14.6 us (7%)
  other arithmetic  14.3 us (7%)
  starting transfers between devices  7.01 us (3%)
  loops' own time  2.85 us (1%)
    psum x1, waiting for transfers between devices, shards(): lax.psum(partial_out.astype(jnp.bfloat16), 'heads').astype(jnp.float32)  35.7 us
    all_gather x1, waiting for transfers between devices, shards(): value_piece = lax.all_gather(values_all, 'bricks', axis=0, tiled=True)  26.8 us
    reduce_scatter x1, waiting for transfers between devices, shards(): lax.psum_scatter(lowered.astype(jnp.bfloat16), 'heads', scatter_dimension...  25.4 us
    all_gather x1, waiting for transfers between devices, shards(): key_piece = lax.all_gather(keys_all, 'bricks', axis=0, tiled=True)  24 us
    all_gather x1, waiting for transfers between devices, shards(): stream_full = lax.all_gather(stream, 'heads', axis=1, tiled=True)  17.6 us
    ppermute x1, starting transfers between devices, extended_2(): before = lax.ppermute(last, axis, up)  5.56 us
    dot_general x1, matrix products, shards(): lowered = jnp.dot(hidden, down_weight, preferred_element_type=jnp.float32)  5.37 us
    dynamic_slice x4, local copies, waits for them, and re-layouts, absorb(): linked = pattern[first_brick + local_id, key_brick]  5.15 us
  transfers between devices with their start and end apart: 7, of which 5 were waited for; matrix products, arithmetic and copies ran while one was open for 5% of the time, Pallas kernels for 0%

commit v1 on v0

--- a/solution.py
+++ b/solution.py
@@ -6,6 +6,28 @@
 EDGE = 8
 HEAD_DIM = 64
 epsilon = 1e-05
+
+
+def joined_along(parts, dim):
+    parts = jnp.moveaxis(parts, 0, dim)
+    lengths = parts.shape
+    return parts.reshape(*lengths[:dim], lengths[dim] * lengths[dim + 1], *lengths[dim + 2 :])
+
+
+def collect(x, axis, dim):
+    size = lax.axis_size(axis)
+    pairs = [(i, (i + 1) % size) for i in range(size)]
+    back = [(b, a) for a, b in pairs]
+    lower, upper = ([], [])
+    for step in range(size - 1):
+        if step % 2 == 0:
+            lower.append(lax.ppermute(lower[-1] if lower else x, axis, pairs))
+        else:
+            upper.append(lax.ppermute(upper[-1] if upper else x, axis, back))
+    blocks = jnp.stack([*lower[::-1], x, *upper])
+    shift = lax.axis_index(axis) - len(lower)
+    blocks = blocks[(jnp.arange(size) - shift) % size]
+    return joined_along(blocks, dim)
 
 
 def extended_2(value, sides, width):
@@ -142,7 +164,7 @@
     values_all = jnp.dot(normed, value_weight, preferred_element_type=jnp.float32).astype(
         jnp.bfloat16
     )
-    key_piece = lax.all_gather(keys_all, "bricks", axis=0, tiled=True)
+    key_piece = collect(keys_all, "bricks", 0)
     value_piece = lax.all_gather(values_all, "bricks", axis=0, tiled=True)
     piece_bricks = key_piece.shape[0] // brick_rows
 

time: 209 us -> 197 us (0.943)
  waiting for transfers between devices: 129 us -> 108 us
  starting transfers between devices: 7.01 us -> 13.6 us
    all_gather x1, waiting for transfers between devices: 26.8 us -> 0.01 us  [shards(): value_piece = lax.all_gather(values_all, 'bricks', axis=0, tiled=True)]
    ppermute x0 -> x3, waiting for transfers between devices: none -> 25.8 us  [the longest x1 13.6 us: collect(): upper.append(lax.ppermute(upper[-1] if upper else x, axis, back))]
    all_gather x1 -> x0, waiting for transfers between devices: 24 us -> none  [shards(): key_piece = lax.all_gather(keys_all, 'bricks', axis=0, tiled=True)]
    ppermute x0 -> x3, starting transfers between devices: none -> 6.63 us  [the longest x2 4.23 us: collect(): lower.append(lax.ppermute(lower[-1] if lower else x, axis, pairs))]
    psum x1, waiting for transfers between devices: 35.7 us -> 38.7 us  [shards(): lax.psum(partial_out.astype(jnp.bfloat16), 'heads').astype(jnp.float32)]
  transfers between devices with their start and end apart: 7 -> 9, of which waited for: 5 -> 6; matrix products, arithmetic and copies ran while one was open for 5% -> 7% of each run, Pallas kernels for 0% -> 0%
where the time goes in v1:
time: 197 us; the launch traced here: 196 us
  waiting for transfers between devices  108 us (55%)
  matrix products  21 us (11%)
  local copies, waits for them, and re-layouts  20.8 us (11%)
  other arithmetic  15.5 us (8%)
  between operations  14.6 us (7%)
  starting transfers between devices  13.6 us (7%)
  loops' own time  2.85 us (1%)
    psum x1, waiting for transfers between devices, shards(): lax.psum(partial_out.astype(jnp.bfloat16), 'heads').astype(jnp.float32)  38.7 us
    reduce_scatter x1, waiting for transfers between devices, shards(): lax.psum_scatter(lowered.astype(jnp.bfloat16), 'heads', scatter_dimension...  25.4 us
    all_gather x1, waiting for transfers between devices, shards(): stream_full = lax.all_gather(stream, 'heads', axis=1, tiled=True)  17.6 us
    ppermute x1, waiting for transfers between devices, collect(): upper.append(lax.ppermute(upper[-1] if upper else x, axis, back))  13.6 us
    ppermute x2, waiting for transfers between devices, collect(): lower.append(lax.ppermute(lower[-1] if lower else x, axis, pairs))  12.2 us
    ppermute x1, starting transfers between devices, extended_2(): before = lax.ppermute(last, axis, up)  5.56 us
    dot_general x1, matrix products, shards(): lowered = jnp.dot(hidden, down_weight, preferred_element_type=jnp.float32)  5.36 us
    dynamic_slice x4, local copies, waits for them, and re-layouts, absorb(): linked = pattern[first_brick + local_id, key_brick]  5.15 us
  transfers between devices with their start and end apart: 9, of which 6 were waited for; matrix products, arithmetic and copies ran while one was open for 7% of the time, Pallas kernels for 0%

profile of v1, /device:TPU:0, one launch (start us, length us, event | category | flops | bytes accessed | tf_op | source)
XLA Modules:
  0.0 196.0 jit_solution(14588108056731772593)
XLA Ops:
  8.8 5.6 %collective-permute-start = (bf16[64,256]{1,0:T(8,128)(2,1)S(1)}, bf16[64,256]{1,0:T(8,128)(2,1)S(1)}, u32[]{:S(2)}, u32[]{:S(2)}) collective-permute-start(bf16[64,256]{1,0:T(8,128)(2,1)S(1)} %get-tuple-element.350), channel_id=1, source_target_pairs={{0,4},{4,8},{8,12},{1,5},{5,9},{9,13},{2,6},{6,10},{10,14},{3,7},{... | collective-permute-start | bytes 98312 | tf_op jit(solution)/shard_map/ppermute | solution.py:40
  16.2 1.4 fusion.100
  20.9 1.6 fusion.57
  23.4 17.6 %all-gather.3.cloned.1.call-done = bf16[512,1024]{1,0:T(8,128)(2,1)} async-done(((bf16[512,256]{1,0:T(8,128)(2,1)}), bf16[512,1024]{1,0:T(8,128)(2,1)}) %all-gather.3.cloned.1.call-update) | async-done | bytes 1048592 | tf_op jit(solution)/shard_map/all_gather | solution.py:117
  41.0 1.5 convert_reduce_fusion
  42.5 1.6 fusion.25
  44.2 2.3 %convolution_convert_fusion.2 = bf16[512,256]{1,0:T(8,128)(2,1)} fusion(bf16[1024,256]{1,0:T(8,128)(2,1)} %param.25, bf16[512,1024]{1,0:T(8,128)(2,1)S(1)} %copy-done.1, f32[1024]{0:T(1024)S(1)} %convert_element_type.108, f32[512]{0:T(512)S(1)} %add_rsqrt_fusion.1, f32[512]{0:T(512)S(1)} %broadcast_multiply_fusion.1), kind=kOutput, calls=%fused_computation.60 | convolution fusion | flops 271187968 | bytes 1843200 | tf_op jit(solution)/shard_map/dot_general | solution.py:164
  46.5 2.3 %convolution_convert_fusion.4 = bf16[512,256]{1,0:T(8,128)(2,1)} fusion(bf16[1024,256]{1,0:T(8,128)(2,1)} %param.24, bf16[512,1024]{1,0:T(8,128)(2,1)S(1)} %copy-done.1, f32[1024]{0:T(1024)S(1)} %convert_element_type.108, f32[512]{0:T(512)S(1)} %add_rsqrt_fusion.1, f32[512]{0:T(512)S(1)} %broadcast_multiply_fusion.1), kind=kOutput, calls=%fused_computation.62 | convolution fusion | flops 271187968 | bytes 1843200 | tf_op jit(solution)/shard_map/dot_general | solution.py:163
  48.8 1.5 collective-permute-start.2
  50.3 2.4 %collective-permute-start.4 = (bf16[512,256]{1,0:T(8,128)(2,1)}, bf16[512,256]{1,0:T(8,128)(2,1)S(1)}, u32[]{:S(2)}, u32[]{:S(2)}) collective-permute-start(bf16[512,256]{1,0:T(8,128)(2,1)} %convolution_convert_fusion.4), channel_id=1, source_target_pairs={{4,0},{8,4},{12,8},{0,12},{5,1},{9,5},{13,9},{1,13},{6,2},{10,6},{... | collective-permute-start | bytes 786440 | tf_op jit(solution)/shard_map/ppermute | solution.py:26
  52.7 8.6 %collective-permute-done.2 = bf16[512,256]{1,0:T(8,128)(2,1)} collective-permute-done((bf16[512,256]{1,0:T(8,128)(2,1)}, bf16[512,256]{1,0:T(8,128)(2,1)}, u32[]{:S(2)}, u32[]{:S(2)}) %collective-permute-start.2) | collective-permute-done | bytes 262176 | tf_op jit(solution)/shard_map/ppermute | solution.py:24
  61.2 2.7 %collective-permute-start.3 = (bf16[512,256]{1,0:T(8,128)(2,1)}, bf16[512,256]{1,0:T(8,128)(2,1)S(1)}, u32[]{:S(2)}, u32[]{:S(2)}) collective-permute-start(bf16[512,256]{1,0:T(8,128)(2,1)} %collective-permute-done.2), channel_id=1, source_target_pairs={{0,4},{4,8},{8,12},{12,0},{1,5},{5,9},{9,13},{13,1},{2,6},{6,10},{... | collective-permute-start | bytes 786440 | tf_op jit(solution)/shard_map/ppermute | solution.py:24
  64.0 1.7 convolution_convert_fusion.3
  65.7 13.6 %collective-permute-done.4 = bf16[512,256]{1,0:T(8,128)(2,1)S(1)} collective-permute-done((bf16[512,256]{1,0:T(8,128)(2,1)}, bf16[512,256]{1,0:T(8,128)(2,1)S(1)}, u32[]{:S(2)}, u32[]{:S(2)}) %collective-permute-start.4) | collective-permute-done | bytes 262176 | tf_op jit(solution)/shard_map/ppermute | solution.py:26
  79.3 3.7 %collective-permute-done.3 = bf16[512,256]{1,0:T(8,128)(2,1)S(1)} collective-permute-done((bf16[512,256]{1,0:T(8,128)(2,1)}, bf16[512,256]{1,0:T(8,128)(2,1)S(1)}, u32[]{:S(2)}, u32[]{:S(2)}) %collective-permute-start.3) | collective-permute-done | bytes 262176 | tf_op jit(solution)/shard_map/ppermute | solution.py:24
  84.1 1.6 gather_fusion
  85.7 2.3 %copy.15 = bf16[2048,256]{0,1:T(8,128)(2,1)} copy(bf16[2048,256]{1,0:T(8,128)(2,1)} %bitcast.122) | data formatting | bytes 2097152 | tf_op jit(solution)/shard_map/while | solution.py:183
  88.0 2.3 %copy.16 = bf16[2048,256]{0,1:T(8,128)(2,1)} copy(bf16[2048,256]{1,0:T(8,128)(2,1)} %all-gather.5.cloned.1.call-done) | data formatting | bytes 2097152 | tf_op jit(solution)/shard_map/while | solution.py:183
  90.3 22.0 %while.21 = (s32[]{:T(128)}, f32[1,4,512]{2,1,0:T(4,128)S(1)}, f32[1,4,512]{2,1,0:T(4,128)S(1)}, f32[1,512,4,64]{1,3,2,0:T(8,128)S(1)}, s32[]{:T(128)}, /*index=...) while((s32[]{:T(128)}, f32[1,4,512]{2,1,0:T(4,128)S(1)}, ...), condition=%wide.region_7.8_spmd, body=%wide.region_2.0_spmd.sunk | while | flops 277094432 | bytes 15589916 | solution.py:183
  90.4 1.3 dynamic_slice.33
  92.3 3.5 %conditional.2 = ((f32[1,4,512]{2,1,0:T(4,128)S(1)}, f32[1,4,512]{2,1,0:T(4,128)S(1)}, f32[1,512,4,64]{1,3,2,0:T(8,128)S(1)})) conditional(s32[]{:T(128)} %bitcast.118, (f32[1,4,512]{2,1,0:T(4,128)S(1)}, f32[1,4,512]{2,1,0:T(4,128)S(1)}, f32[1,512,4,64]{1,3,2,0:T(8,128)S(1)}) %tuple.92, (s32[]{:T(128)}, bf16[2048,256]{0,1:T(8,128)(2,1)}, ...), branch_computations={%region_3.3_spmd, %region_4.6_spmd} | conditional | flops 277094400 | bytes 15589458 | solution.py:161
  95.9 1.3 dynamic_slice.33
  97.8 3.5 %conditional.2 = ((f32[1,4,512]{2,1,0:T(4,128)S(1)}, f32[1,4,512]{2,1,0:T(4,128)S(1)}, f32[1,512,4,64]{1,3,2,0:T(8,128)S(1)})) conditional(s32[]{:T(128)} %bitcast.118, (f32[1,4,512]{2,1,0:T(4,128)S(1)}, f32[1,4,512]{2,1,0:T(4,128)S(1)}, f32[1,512,4,64]{1,3,2,0:T(8,128)S(1)}) %tuple.92, (s32[]{:T(128)}, bf16[2048,256]{0,1:T(8,128)(2,1)}, ...), branch_computations={%region_3.3_spmd, %region_4.6_spmd} | conditional | flops 277094400 | bytes 15589458 | solution.py:161
  101.4 1.3 dynamic_slice.33
  103.3 3.5 %conditional.2 = ((f32[1,4,512]{2,1,0:T(4,128)S(1)}, f32[1,4,512]{2,1,0:T(4,128)S(1)}, f32[1,512,4,64]{1,3,2,0:T(8,128)S(1)})) conditional(s32[]{:T(128)} %bitcast.118, (f32[1,4,512]{2,1,0:T(4,128)S(1)}, f32[1,4,512]{2,1,0:T(4,128)S(1)}, f32[1,512,4,64]{1,3,2,0:T(8,128)S(1)}) %tuple.92, (s32[]{:T(128)}, bf16[2048,256]{0,1:T(8,128)(2,1)}, ...), branch_computations={%region_3.3_spmd, %region_4.6_spmd} | conditional | flops 277094400 | bytes 15589458 | solution.py:161
  108.8 3.5 %conditional.2 = ((f32[1,4,512]{2,1,0:T(4,128)S(1)}, f32[1,4,512]{2,1,0:T(4,128)S(1)}, f32[1,512,4,64]{1,3,2,0:T(8,128)S(1)})) conditional(s32[]{:T(128)} %bitcast.118, (f32[1,4,512]{2,1,0:T(4,128)S(1)}, f32[1,4,512]{2,1,0:T(4,128)S(1)}, f32[1,512,4,64]{1,3,2,0:T(8,128)S(1)}) %tuple.92, (s32[]{:T(128)}, bf16[2048,256]{0,1:T(8,128)(2,1)}, ...), branch_computations={%region_3.3_spmd, %region_4.6_spmd} | conditional | flops 277094400 | bytes 15589458 | solution.py:161
  112.4 2.6 %convolution_convert_fusion.1 = bf16[512,1024]{1,0:T(8,128)(2,1)} fusion(bf16[512,256]{0,1:T(8,128)(2,1)S(1)} %bitcast.124, bf16[256,1024]{1,0:T(8,128)(2,1)} %param.26), kind=kOutput, calls=%fused_computation.59 | convolution fusion | flops 268959744 | bytes 1835008 | tf_op jit(solution)/shard_map/dot_general | solution.py:187
  115.1 38.7 %all-reduce.3.cloned.1.call-done = bf16[512,1024]{1,0:T(8,128)(2,1)} async-done(((bf16[512,1024]{1,0:T(8,128)(2,1)}), bf16[512,1024]{1,0:T(8,128)(2,1)}) %all-reduce.3.cloned.1.call-update) | async-done | bytes 1048592 | tf_op jit(solution)/shard_map/psum | solution.py:188
  153.8 1.6 convert_reduce_fusion.1
  156.8 5.4 %convolution_convert_fusion = bf16[512,1024]{1,0:T(8,128)(2,1)} fusion(bf16[1024,1024]{1,0:T(8,128)(2,1)S(1)} %copy-done, bf16[1024,1024]{1,0:T(8,128)(2,1)} %param.28, bf16[512,1024]{1,0:T(8,128)(2,1)} %copy-done.3, f32[1024]{0:T(1024)S(1)} %convert_element_type.119, f32[512]{0:T(512)S(1)} %add_rsqrt_fusion, f32[512]{0:T(512)S(1)} %broadcast_multiply_fusion), kind=kOutput, calls=%fused_computation.58 | convolution fusion | flops 2155347968 | bytes 6299648 | tf_op jit(solution)/shard_map/dot_general | solution.py:197
  162.2 25.4 %reduce-scatter.2.cloned.1.call-done = bf16[512,256]{1,0:T(8,128)(2,1)} async-done(((bf16[512,1024]{1,0:T(8,128)(2,1)}), bf16[512,256]{1,0:T(8,128)(2,1)}) %reduce-scatter.2.cloned.1.call-update) | async-done | bytes 262160 | tf_op jit(solution)/shard_map/reduce_scatter | solution.py:198
  187.7 1.8 add_convert_fusion
  (74 shorter events, 25.0 us)
Async XLA Ops:
  6.5 150.3 %copy-start = (bf16[1024,1024]{1,0:T(8,128)(2,1)S(1)}, bf16[1024,1024]{1,0:T(8,128)(2,1)}, u32[]{:S(2)}) copy-start(bf16[1024,1024]{1,0:T(8,128)(2,1)} %param.29) | copy-start | bytes 6291460
  6.5 34.4 %all-gather.3.cloned.1.call-start = ((), (), s32[]{:S(2)}) async-start(), calls=%async_computation.1 | async-start | bytes 1310720 | tf_op jit(solution)/shard_map/all_gather | solution.py:117
  7.5 13.1 %collective-permute-start.1 = (bf16[64,256]{1,0:T(8,128)(2,1)S(1)}, bf16[64,256]{1,0:T(8,128)(2,1)S(1)}, u32[]{:S(2)}, u32[]{:S(2)}) collective-permute-start(bf16[64,256]{1,0:T(8,128)(2,1)S(1)} %get-tuple-element.351), channel_id=1, source_target_pairs={{4,0},{8,4},{12,8},{5,1},{9,5},{13,9},{6,2},{10,6},{14,10},{7,3},{... | collective-permute-start | bytes 98312 | tf_op jit(solution)/shard_map/ppermute | solution.py:41
  8.8 11.8 %collective-permute-start = (bf16[64,256]{1,0:T(8,128)(2,1)S(1)}, bf16[64,256]{1,0:T(8,128)(2,1)S(1)}, u32[]{:S(2)}, u32[]{:S(2)}) collective-permute-start(bf16[64,256]{1,0:T(8,128)(2,1)S(1)} %get-tuple-element.350), channel_id=1, source_target_pairs={{0,4},{4,8},{8,12},{1,5},{5,9},{9,13},{2,6},{6,10},{10,14},{3,7},{... | collective-permute-start | bytes 98312 | tf_op jit(solution)/shard_map/ppermute | solution.py:40
  20.9 1.6 copy-start.4
  20.9 2.5 %copy-start.5 = (bf16[1024]{0:T(1024)(128)(2,1)S(1)}, bf16[1024]{0:T(1024)(128)(2,1)}, u32[]{:S(2)}) copy-start(bf16[1024]{0:T(1024)(128)(2,1)} %param.22) | copy-start | bytes 6148
  23.3 64.7 %all-gather.5.cloned.1.call-start = ((), (), s32[]{:S(2)}) async-start(), calls=%async_computation.2 | async-start | bytes 1310720 | tf_op jit(solution)/shard_map/all_gather | solution.py:168
  41.0 3.2 %copy-start.1 = (bf16[512,1024]{1,0:T(8,128)(2,1)S(1)}, bf16[512,1024]{1,0:T(8,128)(2,1)}, u32[]{:S(2)}) copy-start(bf16[512,1024]{1,0:T(8,128)(2,1)} %all-gather.3.cloned.1.call-done) | copy-start | bytes 3145732
  46.4 107.4 %all-reduce.3.cloned.1.call-start = ((), (), s32[]{:S(2)}) async-start(), calls=%async_computation.3 | async-start | bytes 2097152 | tf_op jit(solution)/shard_map/psum | solution.py:188
  48.8 12.5 %collective-permute-start.2 = (bf16[512,256]{1,0:T(8,128)(2,1)}, bf16[512,256]{1,0:T(8,128)(2,1)}, u32[]{:S(2)}, u32[]{:S(2)}) collective-permute-start(bf16[512,256]{1,0:T(8,128)(2,1)} %convolution_convert_fusion.4), channel_id=1, source_target_pairs={{0,4},{4,8},{8,12},{12,0},{1,5},{5,9},{9,13},{13,1},{2,6},{6,10},{... | collective-permute-start | bytes 786440 | tf_op jit(solution)/shard_map/ppermute | solution.py:24
  50.3 29.0 %collective-permute-start.4 = (bf16[512,256]{1,0:T(8,128)(2,1)}, bf16[512,256]{1,0:T(8,128)(2,1)S(1)}, u32[]{:S(2)}, u32[]{:S(2)}) collective-permute-start(bf16[512,256]{1,0:T(8,128)(2,1)} %convolution_convert_fusion.4), channel_id=1, source_target_pairs={{4,0},{8,4},{12,8},{0,12},{5,1},{9,5},{13,9},{1,13},{6,2},{10,6},{... | collective-permute-start | bytes 786440 | tf_op jit(solution)/shard_map/ppermute | solution.py:26
  61.2 21.7 %collective-permute-start.3 = (bf16[512,256]{1,0:T(8,128)(2,1)}, bf16[512,256]{1,0:T(8,128)(2,1)S(1)}, u32[]{:S(2)}, u32[]{:S(2)}) collective-permute-start(bf16[512,256]{1,0:T(8,128)(2,1)} %collective-permute-done.2), channel_id=1, source_target_pairs={{0,4},{4,8},{8,12},{12,0},{1,5},{5,9},{9,13},{13,1},{2,6},{6,10},{... | collective-permute-start | bytes 786440 | tf_op jit(solution)/shard_map/ppermute | solution.py:24
  112.3 2.7 %copy-start.6 = (bf16[1024]{0:T(1024)(128)(2,1)S(1)}, bf16[1024]{0:T(1024)(128)(2,1)}, u32[]{:S(2)}) copy-start(bf16[1024]{0:T(1024)(128)(2,1)} %param.27) | copy-start | bytes 6148
  112.4 41.4 %copy-start.2 = (bf16[512,1024]{1,0:T(8,128)(2,1)S(1)}, bf16[512,1024]{1,0:T(8,128)(2,1)}, u32[]{:S(2)}) copy-start(bf16[512,1024]{1,0:T(8,128)(2,1)} %all-gather.3.cloned.1.call-done) | copy-start | bytes 3145732
  115.0 72.7 %reduce-scatter.2.cloned.1.call-start = ((), (), s32[]{:S(2)}) async-start(), calls=%async_computation.4 | async-start | bytes 1310720 | tf_op jit(solution)/shard_map/reduce_scatter | solution.py:198
  155.4 1.0 copy-start.3
Sparse Core Ops, SparseCore 0:
  23.4 17.5 all-gather.2
  46.6 41.0 all-gather.4
  115.1 38.6 all-reduce.2
  162.3 25.2 reduce-scatter.1
